TPU v7x, 32 devices: a whole 2x2x4 slice. The times are simulated.
32 devices in a mesh: groups: 2 (over y), ctx: 4 (over z), fsdp: 2 (over x), sub: 2 (over core).
Axes of the slice: x: 2, y: 2, z: 4, core: 2. Of those that a mesh axis runs over, the one named last changes fastest.
Arguments:
- layer_input: bfloat16 [4, 2048, 2304], P(('groups', 'fsdp'), ('ctx', 'sub')), parts along dimension 0, may hold values from -6 to 6
- query_heads: bfloat16 [4, 2048, 1024], P(('groups', 'fsdp'), ('ctx', 'sub')), parts along dimension 0, may hold values from -11 to 11
- key_heads: bfloat16 [4, 2048, 512], P(('groups', 'fsdp'), ('ctx', 'sub')), parts along dimension 0, may hold values from -11 to 11
- value_heads: bfloat16 [4, 2048, 512], P(('groups', 'fsdp'), ('ctx', 'sub')), parts along dimension 0, may hold values from -6 to 6
- grad_out: bfloat16 [4, 2048, 1024], P(('groups', 'fsdp'), ('ctx', 'sub')), parts along dimension 0, may hold values from -96 to 96
- doc_starts: int32 [4, 12], P(('groups', 'fsdp')), parts along dimension 0, may hold values from 0 to 2047, as said below
Outputs:
- grad_query: bfloat16 [4, 2048, 1024], P(('groups', 'fsdp'), ('ctx', 'sub')), parts along dimension 0
- grad_key: bfloat16 [4, 2048, 512], P(('groups', 'fsdp'), ('ctx', 'sub')), parts along dimension 0
- grad_value: bfloat16 [4, 2048, 512], P(('groups', 'fsdp'), ('ctx', 'sub')), parts along dimension 0
- grad_value_proj: float32 [4608, 512], P(('groups', 'fsdp')), parts along dimension 0
There are 2 independent parts, one for each index of `groups`. A program takes and returns all parts, laid end to end along the dimension named above; each array names one. Nothing has to cross between parts.
Inputs may be any that keep to these rules, and one draw needn't show every extreme that they name: `doc_starts`: each row holds the first positions of the 12 documents of one sequence in increasing order; the first is 0, every document has at least one token, and the longest has exactly 1024 tokens.
All inputs are finite; a program needn't handle non-finite values.
Results may differ from a plain program's by a relative error of at most 0.015.
Values may be sent and summed in bfloat16 or wider, within the bound.
No kernel may reach another device: no remote copies, remote signals or barrier semaphores. Data moves between devices by JAX's collectives and lax.ppermute only.
A program may use at most 64 MiB of HBM per device.

v0:
```python
import jax
import jax.numpy as jnp
from jax import lax
from jax.sharding import PartitionSpec as P

HEAD_DIM = 256
SPAN = 768


def passed_along(value, axis, steps):
    count = lax.axis_size(axis)
    first, last = (max(0, -steps), min(count, count - steps))
    return lax.ppermute(value, axis, [(source, source + steps) for source in range(first, last)])


def doc_start_of(starts, positions):
    covered = starts[None, :] <= positions[:, None]
    return jnp.max(jnp.where(covered, starts[None, :], 0), axis=1)


def attend_block(queries, key_block, value_block, grads, query_pos, key_pos, lowest):
    row_count = queries.shape[0]
    key_count = key_block.shape[0]
    groups = key_block.shape[1] // HEAD_DIM
    per_group = queries.shape[1] // key_block.shape[1]
    inv_root = HEAD_DIM ** (-0.5)
    query_four = queries.reshape(row_count, groups, per_group, HEAD_DIM)
    grad_four = grads.reshape(row_count, groups, per_group, HEAD_DIM)
    key_three = key_block.reshape(key_count, groups, HEAD_DIM)
    value_three = value_block.reshape(key_count, groups, HEAD_DIM)
    allowed = (key_pos[None, :] >= lowest[:, None]) & (key_pos[None, :] <= query_pos[:, None])

    def one_group(group):
        query_g = lax.dynamic_index_in_dim(query_four, group, 1, keepdims=False)
        grad_g = lax.dynamic_index_in_dim(grad_four, group, 1, keepdims=False)
        key_g = lax.dynamic_index_in_dim(key_three, group, 1, keepdims=False)
        value_g = lax.dynamic_index_in_dim(value_three, group, 1, keepdims=False)
        scores = (
            jnp.einsum("thd,kd->htk", query_g, key_g, preferred_element_type=jnp.float32) * inv_root
        )
        scores = jnp.where(allowed[None], scores, -1e30)
        largest = jnp.max(scores, axis=2, keepdims=True)
        raised = jnp.where(allowed[None], jnp.exp(scores - largest), 0.0)
        attn_probs = raised / jnp.sum(raised, axis=2, keepdims=True)
        grad_probs = jnp.einsum("thd,kd->htk", grad_g, value_g, preferred_element_type=jnp.float32)
        row_dot = jnp.sum(attn_probs * grad_probs, axis=2, keepdims=True)
        grad_scores = (attn_probs * (grad_probs - row_dot) * inv_root).astype(jnp.bfloat16)
        probs_low = attn_probs.astype(jnp.bfloat16)
        grad_q = jnp.einsum("htk,kd->thd", grad_scores, key_g, preferred_element_type=jnp.float32)
        grad_k = jnp.einsum("htk,thd->kd", grad_scores, query_g, preferred_element_type=jnp.float32)
        grad_v = jnp.einsum("htk,thd->kd", probs_low, grad_g, preferred_element_type=jnp.float32)
        return (grad_q, grad_k, grad_v)

    grad_q, grad_k, grad_v = lax.map(one_group, jnp.arange(groups, dtype=jnp.int32))
    grad_q = jnp.moveaxis(grad_q, 0, 1).reshape(row_count, -1)
    grad_k = jnp.moveaxis(grad_k, 0, 1).reshape(key_count, -1)
    grad_v = jnp.moveaxis(grad_v, 0, 1).reshape(key_count, -1)
    return (grad_q, grad_k, grad_v)


def body(layer_input, query_heads, key_heads, value_heads, grad_out, doc_starts):
    block_rows = query_heads.shape[1]
    window = min(SPAN, lax.axis_size(("ctx", "sub")) * block_rows // 2)
    reach_blocks = (window + block_rows - 2) // block_rows
    margin_rows = reach_blocks * block_rows
    key_count = margin_rows + block_rows
    first_row = lax.axis_index(("ctx", "sub")) * block_rows
    own_keys = key_heads[0]
    own_values = value_heads[0]
    arrived = []
    moving_k = own_keys
    moving_v = own_values
    for distance in range(reach_blocks):
        moving_k, moving_v = passed_along((moving_k, moving_v), ("ctx", "sub"), 1)
        arrived.append((moving_k, moving_v))
    arrived = arrived[::-1]
    key_span = jnp.concatenate([pair[0] for pair in arrived] + [own_keys], axis=0)
    value_span = jnp.concatenate([pair[1] for pair in arrived] + [own_values], axis=0)
    query_pos = first_row + jnp.arange(block_rows, dtype=jnp.int32)
    key_pos = first_row - margin_rows + jnp.arange(key_count, dtype=jnp.int32)
    lowest = jnp.maximum(doc_start_of(doc_starts[0], query_pos), query_pos - window + 1)
    grad_q, grad_k_span, grad_v_span = attend_block(
        query_heads[0], key_span, value_span, grad_out[0], query_pos, key_pos, lowest
    )

    def own_piece(distance):
        begin = (reach_blocks - distance) * block_rows
        return (grad_k_span[begin : begin + block_rows], grad_v_span[begin : begin + block_rows])

    total_k, total_v = own_piece(reach_blocks)
    for distance in range(reach_blocks - 1, -1, -1):
        moved_k, moved_v = (
            passed_along(total_k.astype(jnp.bfloat16), ("ctx", "sub"), -1).astype(total_k.dtype),
            passed_along(total_v.astype(jnp.bfloat16), ("ctx", "sub"), -1).astype(total_v.dtype),
        )
        piece_k, piece_v = own_piece(distance)
        total_k = moved_k + piece_k
        total_v = moved_v + piece_v
    grad_key = total_k.astype(jnp.bfloat16)
    grad_value = total_v.astype(jnp.bfloat16)
    contract = (((0,), (0,)), ((), ()))
    term_v = lax.dot_general(
        layer_input[0], grad_value, contract, preferred_element_type=jnp.float32
    )
    shard_v = lax.psum_scatter(term_v.astype(jnp.bfloat16), "fsdp", scatter_dimension=0, tiled=True)
    weight_v = lax.psum(shard_v, ("ctx", "sub")).astype(jnp.float32)
    token_scale = float(lax.axis_size("fsdp") * lax.axis_size(("ctx", "sub")) * block_rows) ** (
        -0.5
    )
    return (
        grad_q.astype(jnp.bfloat16)[None],
        grad_key[None],
        grad_value[None],
        weight_v * token_scale,
    )


def solution(mesh):
    placed = (
        P(("groups", "fsdp"), ("ctx", "sub"), None),
        P(("groups", "fsdp"), ("ctx", "sub"), None),
        P(("groups", "fsdp"), ("ctx", "sub"), None),
        P(("groups", "fsdp"), ("ctx", "sub"), None),
        P(("groups", "fsdp"), ("ctx", "sub"), None),
        P(("groups", "fsdp"), None),
    )
    return jax.shard_map(
        body,
        mesh=mesh,
        in_specs=placed,
        out_specs=(
            P(("groups", "fsdp"), ("ctx", "sub"), None),
            P(("groups", "fsdp"), ("ctx", "sub"), None),
            P(("groups", "fsdp"), ("ctx", "sub"), None),
            P(("groups", "fsdp"), None),
        ),
        check_vma=False,
    )
```

profile of v0, /device:TPU:0, one launch (start us, length us, event | category | flops | bytes accessed | tf_op | source)
XLA Modules:
  0.0 211.9 jit_solution(1971740638180802092)
XLA Ops:
  7.2 1.2 copy.68
  8.4 2.4 %collective-permute-start = (bf16[256,512]{0,1:T(8,128)(2,1)S(1)}, bf16[256,512]{0,1:T(8,128)(2,1)S(1)}, u32[]{:S(2)}, u32[]{:S(2)}) collective-permute-start(bf16[256,512]{0,1:T(8,128)(2,1)S(1)} %bitcast.186), channel_id=1, source_target_pairs={{0,1},{1,4},{4,5},{5,8},{8,9},{9,12},{12,13},{2,3},{3,6},{6,7},{7,... | collective-permute-start | bytes 786440 | tf_op jit(solution)/shard_map/ppermute | solution.py:13
  10.8 1.1 copy.71
  11.9 4.6 %collective-permute-start.3 = (bf16[256,512]{0,1:T(8,128)(2,1)S(1)}, bf16[256,512]{0,1:T(8,128)(2,1)S(1)}, u32[]{:S(2)}, u32[]{:S(2)}) collective-permute-start(bf16[256,512]{0,1:T(8,128)(2,1)S(1)} %bitcast.184), channel_id=1, source_target_pairs={{0,1},{1,4},{4,5},{5,8},{8,9},{9,12},{12,13},{2,3},{3,6},{6,7},{7,... | collective-permute-start | bytes 786440 | tf_op jit(solution)/shard_map/ppermute | solution.py:13
  16.5 2.2 %collective-permute-start.1 = (bf16[256,512]{0,1:T(8,128)(2,1)S(1)}, bf16[256,512]{0,1:T(8,128)(2,1)S(1)}, u32[]{:S(2)}, u32[]{:S(2)}) collective-permute-start(bf16[256,512]{0,1:T(8,128)(2,1)S(1)} %collective-permute-done), channel_id=1, source_target_pairs={{0,1},{1,4},{4,5},{5,8},{8,9},{9,12},{12,13},{2,3},{3,6},{6,7},{7,... | collective-permute-start | bytes 786440 | tf_op jit(solution)/shard_map/ppermute | solution.py:13
  18.7 4.4 %collective-permute-start.4 = (bf16[256,512]{0,1:T(8,128)(2,1)S(1)}, bf16[256,512]{0,1:T(8,128)(2,1)S(1)}, u32[]{:S(2)}, u32[]{:S(2)}) collective-permute-start(bf16[256,512]{0,1:T(8,128)(2,1)S(1)} %collective-permute-done.3), channel_id=1, source_target_pairs={{0,1},{1,4},{4,5},{5,8},{8,9},{9,12},{12,13},{2,3},{3,6},{6,7},{7,... | collective-permute-start | bytes 786440 | tf_op jit(solution)/shard_map/ppermute | solution.py:13
  23.9 3.7 %collective-permute-start.2 = (bf16[256,512]{0,1:T(8,128)(2,1)S(1)}, bf16[256,512]{0,1:T(8,128)(2,1)}, u32[]{:S(2)}, u32[]{:S(2)}) collective-permute-start(bf16[256,512]{0,1:T(8,128)(2,1)S(1)} %collective-permute-done.1), channel_id=1, source_target_pairs={{0,1},{1,4},{4,5},{5,8},{8,9},{9,12},{12,13},{2,3},{3,6},{6,7},{7,... | collective-permute-start | bytes 786440 | tf_op jit(solution)/shard_map/ppermute | solution.py:13
  27.6 3.2 %collective-permute-start.5 = (bf16[256,512]{0,1:T(8,128)(2,1)S(1)}, bf16[256,512]{0,1:T(8,128)(2,1)S(1)}, u32[]{:S(2)}, u32[]{:S(2)}) collective-permute-start(bf16[256,512]{0,1:T(8,128)(2,1)S(1)} %collective-permute-done.4), channel_id=1, source_target_pairs={{0,1},{1,4},{4,5},{5,8},{8,9},{9,12},{12,13},{2,3},{3,6},{6,7},{7,... | collective-permute-start | bytes 786440 | tf_op jit(solution)/shard_map/ppermute | solution.py:13
  30.8 2.1 copy.73
  32.9 1.0 copy.70
  33.9 2.1 pad_maximum_fusion
  36.0 1.2 pad_maximum_fusion.1
  37.1 37.4 %while.15 = (s32[]{:T(128)}, bf16[2,256,2,256]{1,3,2,0:T(8,128)(2,1)}, f32[2,1024,256]{2,1,0:T(8,128)}, f32[2,1024,256]{2,1,0:T(8,128)}, s32[2]{0:T(128)S(1)}, /...) while((s32[]{:T(128)}, ...), condition=%wide.region_5.6_spmd.clone, body=%wide.region_1.5_spmd.clone.sunk | while | flops 1353977856 | bytes 29120200 | solution.py:54
  39.9 3.5 %fusion.90 = (f32[2,256]{1,0:T(2,128)S(1)}, f32[2,256,1024]{1,2,0:T(8,128)}) fusion(pred[256,1024]{0,1:T(8,128)(4,1)S(1)} %compare_and_fusion.2, bf16[256,2,2,256]{0,3,2,1:T(8,128)(2,1)} %get-tuple-element.287, s32[]{:T(128)S(6)} %select_n.34, bf16[1024,2,256]{0,2,1:T(8,128)(2,1)} %get-tuple-element.286), kind=kOutput, calls=%fused_computation.80.clone.1 | convolution fusion | flops 271057920 | bytes 3410944 | tf_op jit(solution)/shard_map/while/body/eval_jaxpr/sub | solution.py:43
  43.4 1.6 fusion.89
  45.0 3.9 %fusion.92 = f32[2,1024,256]{2,1,0:T(8,128)} fusion(f32[2,1024,256]{2,1,0:T(8,128)} %get-tuple-element.268, s32[]{:T(128)} %get-tuple-element.266, f32[1024,256,2]{1,0,2:T(8,128)S(1)} %fusion.89, bf16[256,2,2,256]{0,3,2,1:T(8,128)(2,1)} %get-tuple-element.287, s32[]{:T(128)S(6)} %select_n.34, f32[2,256,1024]{1,2,0:T(8,128)} %get-tuple-element.249, ...), kind=kOutput, calls=%fused_computation.14.clone.1 | convolution fusion | flops 272107008 | bytes 9703940 | tf_op jit(solution)/shard_map/while/body/eval_jaxpr/htk,thd->kd/dot_general | solution.py:50
  48.9 3.0 %fusion.93 = f32[2,1024,256]{2,1,0:T(8,128)} fusion(f32[2,1024,256]{2,1,0:T(8,128)} %get-tuple-element.269, s32[]{:T(128)} %get-tuple-element.266, bf16[256,2,2,256]{0,3,2,1:T(8,128)(2,1)} %get-tuple-element.289, s32[]{:T(128)S(6)} %select_n.34, f32[2,256,1024]{1,2,0:T(8,128)} %get-tuple-element.249, f32[2,256]{1,0:T(2,128)S(1)} %get-tuple-element.250), kind=kOutput, calls=%fused_computation.12.clone.1 | convolution fusion | flops 269484032 | bytes 3410436 | tf_op jit(solution)/shard_map/while/body/eval_jaxpr/htk,thd->kd/dot_general | solution.py:51
  51.9 3.9 %fusion.91 = bf16[2,256,2,256]{1,3,2,0:T(8,128)(2,1)} fusion(bf16[2,256,2,256]{1,3,2,0:T(8,128)(2,1)} %get-tuple-element.267, s32[]{:T(128)} %get-tuple-element.266, f32[1024,256,2]{1,0,2:T(8,128)S(1)} %fusion.89, bf16[1024,2,256]{0,2,1:T(8,128)(2,1)} %get-tuple-element.286, s32[]{:T(128)S(6)} %select_n.34, f32[2,256,1024]{1,2,0:T(8,128)} %get-tuple-element.249, ...), kind=kOutput, calls=%fused_computation.16.clone.1 | convolution fusion | flops 272107008 | bytes 9441796 | tf_op jit(solution)/shard_map/while/body/eval_jaxpr/htk,kd->thd/dot_general | solution.py:49
  58.6 3.5 %fusion.90 = (f32[2,256]{1,0:T(2,128)S(1)}, f32[2,256,1024]{1,2,0:T(8,128)}) fusion(pred[256,1024]{0,1:T(8,128)(4,1)S(1)} %compare_and_fusion.2, bf16[256,2,2,256]{0,3,2,1:T(8,128)(2,1)} %get-tuple-element.287, s32[]{:T(128)S(6)} %select_n.34, bf16[1024,2,256]{0,2,1:T(8,128)(2,1)} %get-tuple-element.286), kind=kOutput, calls=%fused_computation.80.clone.1 | convolution fusion | flops 271057920 | bytes 3410944 | tf_op jit(solution)/shard_map/while/body/eval_jaxpr/sub | solution.py:43
  62.1 1.6 fusion.89
  63.6 4.0 %fusion.92 = f32[2,1024,256]{2,1,0:T(8,128)} fusion(f32[2,1024,256]{2,1,0:T(8,128)} %get-tuple-element.268, s32[]{:T(128)} %get-tuple-element.266, f32[1024,256,2]{1,0,2:T(8,128)S(1)} %fusion.89, bf16[256,2,2,256]{0,3,2,1:T(8,128)(2,1)} %get-tuple-element.287, s32[]{:T(128)S(6)} %select_n.34, f32[2,256,1024]{1,2,0:T(8,128)} %get-tuple-element.249, ...), kind=kOutput, calls=%fused_computation.14.clone.1 | convolution fusion | flops 272107008 | bytes 9703940 | tf_op jit(solution)/shard_map/while/body/eval_jaxpr/htk,thd->kd/dot_general | solution.py:50
  67.6 3.0 %fusion.93 = f32[2,1024,256]{2,1,0:T(8,128)} fusion(f32[2,1024,256]{2,1,0:T(8,128)} %get-tuple-element.269, s32[]{:T(128)} %get-tuple-element.266, bf16[256,2,2,256]{0,3,2,1:T(8,128)(2,1)} %get-tuple-element.289, s32[]{:T(128)S(6)} %select_n.34, f32[2,256,1024]{1,2,0:T(8,128)} %get-tuple-element.249, f32[2,256]{1,0:T(2,128)S(1)} %get-tuple-element.250), kind=kOutput, calls=%fused_computation.12.clone.1 | convolution fusion | flops 269484032 | bytes 3410436 | tf_op jit(solution)/shard_map/while/body/eval_jaxpr/htk,thd->kd/dot_general | solution.py:51
  70.7 3.9 %fusion.91 = bf16[2,256,2,256]{1,3,2,0:T(8,128)(2,1)} fusion(bf16[2,256,2,256]{1,3,2,0:T(8,128)(2,1)} %get-tuple-element.267, s32[]{:T(128)} %get-tuple-element.266, f32[1024,256,2]{1,0,2:T(8,128)S(1)} %fusion.89, bf16[1024,2,256]{0,2,1:T(8,128)(2,1)} %get-tuple-element.286, s32[]{:T(128)S(6)} %select_n.34, f32[2,256,1024]{1,2,0:T(8,128)} %get-tuple-element.249, ...), kind=kOutput, calls=%fused_computation.16.clone.1 | convolution fusion | flops 272107008 | bytes 9441796 | tf_op jit(solution)/shard_map/while/body/eval_jaxpr/htk,kd->thd/dot_general | solution.py:49
  74.5 1.1 fusion.61
  75.6 1.3 collective-permute-start.9
  76.9 1.5 slice_bitcast_fusion.2
  78.5 1.2 collective-permute-done.9
  79.7 1.3 collective-permute-start.10
  81.1 6.3 %collective-permute-done.10 = bf16[256,512]{1,0:T(8,128)(2,1)S(1)} collective-permute-done((bf16[256,512]{1,0:T(8,128)(2,1)S(1)}, bf16[256,512]{1,0:T(8,128)(2,1)S(1)}, u32[]{:S(2)}, u32[]{:S(2)}) %collective-permute-start.10) | collective-permute-done | bytes 262176 | tf_op jit(solution)/shard_map/ppermute | solution.py:13
  87.5 1.3 collective-permute-start.11
  88.9 6.3 %collective-permute-done.11 = bf16[256,512]{1,0:T(8,128)(2,1)S(1)} collective-permute-done((bf16[256,512]{1,0:T(8,128)(2,1)S(1)}, bf16[256,512]{1,0:T(8,128)(2,1)S(1)}, u32[]{:S(2)}, u32[]{:S(2)}) %collective-permute-start.11) | collective-permute-done | bytes 262176 | tf_op jit(solution)/shard_map/ppermute | solution.py:13
  95.9 0.8 fusion.57
  96.7 2.4 %copy.92 = bf16[2304,512]{1,0:T(8,128)(2,1)} copy(bf16[2304,512]{0,1:T(8,128)(2,1)S(1)} %fusion.57) | data formatting | bytes 4718592
  99.2 1.1 fusion.60
  100.4 1.3 collective-permute-start.6
  101.7 1.5 slice_bitcast_fusion.5
  103.2 4.9 %collective-permute-done.6 = bf16[256,512]{1,0:T(8,128)(2,1)S(1)} collective-permute-done((bf16[256,512]{1,0:T(8,128)(2,1)S(1)}, bf16[256,512]{1,0:T(8,128)(2,1)S(1)}, u32[]{:S(2)}, u32[]{:S(2)}) %collective-permute-start.6) | collective-permute-done | bytes 262176 | tf_op jit(solution)/shard_map/ppermute | solution.py:13
  108.0 0.8 add_convert_fusion.5
  108.8 1.3 collective-permute-start.7
  110.2 28.5 %reduce-scatter.4.cloned.1.call-done = bf16[1152,512]{1,0:T(8,128)(2,1)} async-done(((bf16[2304,512]{1,0:T(8,128)(2,1)}), bf16[1152,512]{1,0:T(8,128)(2,1)}) %reduce-scatter.4.cloned.1.call-update) | async-done | bytes 1179664
  138.7 2.4 %copy.93 = bf16[1152,512]{0,1:T(8,128)(2,1)} copy(bf16[1152,512]{1,0:T(8,128)(2,1)} %reduce-scatter.4.cloned.1.call-done) | data formatting | bytes 2359296
  141.1 1.8 add_convert_fusion.4
  142.9 1.3 collective-permute-start.8
  144.3 1.0 copy.90
  146.7 1.7 fusion.59
  148.4 53.2 %all-reduce.2.cloned.1.call-done = bf16[1152,512]{0,1:T(8,128)(2,1)} async-done(((bf16[1152,512]{0,1:T(8,128)(2,1)}), bf16[1152,512]{0,1:T(8,128)(2,1)}) %all-reduce.2.cloned.1.call-update) | async-done | bytes 1179664 | tf_op jit(solution)/shard_map/psum | solution.py:106
  201.6 1.4 convert_multiply_fusion
  203.1 2.0 copy.87
  (49 shorter events, 5.2 us)
Async XLA Ops:
  7.2 88.7 %copy-start = (bf16[1,256,2304]{2,1,0:T(8,128)(2,1)S(1)}, bf16[1,256,2304]{2,1,0:T(8,128)(2,1)}, u32[]{:S(2)}) copy-start(bf16[1,256,2304]{2,1,0:T(8,128)(2,1)} %param.8) | copy-start | bytes 3538948
  7.2 25.7 %copy-start.5 = (bf16[1,256,1024]{2,1,0:T(8,128)(2,1)S(1)}, bf16[1,256,1024]{2,1,0:T(8,128)(2,1)}, u32[]{:S(2)}) copy-start(bf16[1,256,1024]{2,1,0:T(8,128)(2,1)} %param.9) | copy-start | bytes 1572868
  7.2 131.5 %reduce-scatter.4.cloned.1.call-start = ((), (), s32[]{:S(2)}) async-start(), calls=%async_computation.2 | async-start | bytes 3538944
  8.4 8.1 %collective-permute-start = (bf16[256,512]{0,1:T(8,128)(2,1)S(1)}, bf16[256,512]{0,1:T(8,128)(2,1)S(1)}, u32[]{:S(2)}, u32[]{:S(2)}) collective-permute-start(bf16[256,512]{0,1:T(8,128)(2,1)S(1)} %bitcast.186), channel_id=1, source_target_pairs={{0,1},{1,4},{4,5},{5,8},{8,9},{9,12},{12,13},{2,3},{3,6},{6,7},{7,... | collective-permute-start | bytes 786440 | tf_op jit(solution)/shard_map/ppermute | solution.py:13
  11.9 6.8 %collective-permute-start.3 = (bf16[256,512]{0,1:T(8,128)(2,1)S(1)}, bf16[256,512]{0,1:T(8,128)(2,1)S(1)}, u32[]{:S(2)}, u32[]{:S(2)}) collective-permute-start(bf16[256,512]{0,1:T(8,128)(2,1)S(1)} %bitcast.184), channel_id=1, source_target_pairs={{0,1},{1,4},{4,5},{5,8},{8,9},{9,12},{12,13},{2,3},{3,6},{6,7},{7,... | collective-permute-start | bytes 786440 | tf_op jit(solution)/shard_map/ppermute | solution.py:13
  16.5 7.4 %collective-permute-start.1 = (bf16[256,512]{0,1:T(8,128)(2,1)S(1)}, bf16[256,512]{0,1:T(8,128)(2,1)S(1)}, u32[]{:S(2)}, u32[]{:S(2)}) collective-permute-start(bf16[256,512]{0,1:T(8,128)(2,1)S(1)} %collective-permute-done), channel_id=1, source_target_pairs={{0,1},{1,4},{4,5},{5,8},{8,9},{9,12},{12,13},{2,3},{3,6},{6,7},{7,... | collective-permute-start | bytes 786440 | tf_op jit(solution)/shard_map/ppermute | solution.py:13
  18.7 8.9 %collective-permute-start.4 = (bf16[256,512]{0,1:T(8,128)(2,1)S(1)}, bf16[256,512]{0,1:T(8,128)(2,1)S(1)}, u32[]{:S(2)}, u32[]{:S(2)}) collective-permute-start(bf16[256,512]{0,1:T(8,128)(2,1)S(1)} %collective-permute-done.3), channel_id=1, source_target_pairs={{0,1},{1,4},{4,5},{5,8},{8,9},{9,12},{12,13},{2,3},{3,6},{6,7},{7,... | collective-permute-start | bytes 786440 | tf_op jit(solution)/shard_map/ppermute | solution.py:13
  23.9 10.0 %collective-permute-start.2 = (bf16[256,512]{0,1:T(8,128)(2,1)S(1)}, bf16[256,512]{0,1:T(8,128)(2,1)}, u32[]{:S(2)}, u32[]{:S(2)}) collective-permute-start(bf16[256,512]{0,1:T(8,128)(2,1)S(1)} %collective-permute-done.1), channel_id=1, source_target_pairs={{0,1},{1,4},{4,5},{5,8},{8,9},{9,12},{12,13},{2,3},{3,6},{6,7},{7,... | collective-permute-start | bytes 786440 | tf_op jit(solution)/shard_map/ppermute | solution.py:13
  27.6 8.4 %collective-permute-start.5 = (bf16[256,512]{0,1:T(8,128)(2,1)S(1)}, bf16[256,512]{0,1:T(8,128)(2,1)S(1)}, u32[]{:S(2)}, u32[]{:S(2)}) collective-permute-start(bf16[256,512]{0,1:T(8,128)(2,1)S(1)} %collective-permute-done.4), channel_id=1, source_target_pairs={{0,1},{1,4},{4,5},{5,8},{8,9},{9,12},{12,13},{2,3},{3,6},{6,7},{7,... | collective-permute-start | bytes 786440 | tf_op jit(solution)/shard_map/ppermute | solution.py:13
  75.6 4.0 %collective-permute-start.9 = (bf16[256,512]{1,0:T(8,128)(2,1)S(1)}, bf16[256,512]{1,0:T(8,128)(2,1)S(1)}, u32[]{:S(2)}, u32[]{:S(2)}) collective-permute-start(bf16[256,512]{1,0:T(8,128)(2,1)S(1)} %bitcast.189), channel_id=1, source_target_pairs={{1,0},{4,1},{5,4},{8,5},{9,8},{12,9},{13,12},{3,2},{6,3},{7,6},{10... | collective-permute-start | bytes 786440 | tf_op jit(solution)/shard_map/ppermute | solution.py:13
  79.7 7.7 %collective-permute-start.10 = (bf16[256,512]{1,0:T(8,128)(2,1)S(1)}, bf16[256,512]{1,0:T(8,128)(2,1)S(1)}, u32[]{:S(2)}, u32[]{:S(2)}) collective-permute-start(bf16[256,512]{1,0:T(8,128)(2,1)S(1)} %add_convert_fusion.2), channel_id=1, source_target_pairs={{1,0},{4,1},{5,4},{8,5},{9,8},{12,9},{13,12},{3,2},{6,3},{7,6},{10... | collective-permute-start | bytes 786440 | tf_op jit(solution)/shard_map/ppermute | solution.py:13
  87.5 7.7 %collective-permute-start.11 = (bf16[256,512]{1,0:T(8,128)(2,1)S(1)}, bf16[256,512]{1,0:T(8,128)(2,1)S(1)}, u32[]{:S(2)}, u32[]{:S(2)}) collective-permute-start(bf16[256,512]{1,0:T(8,128)(2,1)S(1)} %add_convert_fusion.1), channel_id=1, source_target_pairs={{1,0},{4,1},{5,4},{8,5},{9,8},{12,9},{13,12},{3,2},{6,3},{7,6},{10... | collective-permute-start | bytes 786440 | tf_op jit(solution)/shard_map/ppermute | solution.py:13
  88.9 6.3 %copy-start.1 = (f32[2,32,8,256]{3,2,0,1:T(8,128)}, f32[2,32,8,256]{3,2,0,1:T(8,128)S(1)}, u32[]{:S(2)}) copy-start(f32[2,32,8,256]{3,2,0,1:T(8,128)S(1)} %copy.105) | copy-start | bytes 1572868
  95.2 0.7 copy-start.3
  99.2 102.4 %all-reduce.2.cloned.1.call-start = ((), (), s32[]{:S(2)}) async-start(), calls=%async_computation.1 | async-start | bytes 2359296 | tf_op jit(solution)/shard_map/psum | solution.py:106
  100.4 7.7 %collective-permute-start.6 = (bf16[256,512]{1,0:T(8,128)(2,1)S(1)}, bf16[256,512]{1,0:T(8,128)(2,1)S(1)}, u32[]{:S(2)}, u32[]{:S(2)}) collective-permute-start(bf16[256,512]{1,0:T(8,128)(2,1)S(1)} %bitcast.190), channel_id=1, source_target_pairs={{1,0},{4,1},{5,4},{8,5},{9,8},{12,9},{13,12},{3,2},{6,3},{7,6},{10... | collective-permute-start | bytes 786440 | tf_op jit(solution)/shard_map/ppermute | solution.py:13
  108.8 32.3 %collective-permute-start.7 = (bf16[256,512]{1,0:T(8,128)(2,1)}, bf16[256,512]{1,0:T(8,128)(2,1)}, u32[]{:S(2)}, u32[]{:S(2)}) collective-permute-start(bf16[256,512]{1,0:T(8,128)(2,1)} %add_convert_fusion.5), channel_id=1, source_target_pairs={{1,0},{4,1},{5,4},{8,5},{9,8},{12,9},{13,12},{3,2},{6,3},{7,6},{10... | collective-permute-start | bytes 786440 | tf_op jit(solution)/shard_map/ppermute | solution.py:13
  141.1 3.2 %copy-start.6 = (bf16[2,256,2,256]{1,3,2,0:T(8,128)(2,1)S(1)}, bf16[2,256,2,256]{1,3,2,0:T(8,128)(2,1)}, u32[]{:S(2)}) copy-start(bf16[2,256,2,256]{1,3,2,0:T(8,128)(2,1)} %get-tuple-element.58) | copy-start | bytes 1572868
  141.1 4.2 %copy-start.2 = (f32[2,32,8,256]{3,2,0,1:T(8,128)S(1)}, f32[2,32,8,256]{3,2,0,1:T(8,128)}, u32[]{:S(2)}) copy-start(f32[2,32,8,256]{3,2,0,1:T(8,128)} %copy-done.1) | copy-start | bytes 1572868
  141.1 4.2 %copy-start.4 = (bf16[256,512]{1,0:T(8,128)(2,1)S(1)}, bf16[256,512]{1,0:T(8,128)(2,1)}, u32[]{:S(2)}) copy-start(bf16[256,512]{1,0:T(8,128)(2,1)} %copy-done.3) | copy-start | bytes 786436
  142.9 3.8 %collective-permute-start.8 = (bf16[256,512]{1,0:T(8,128)(2,1)}, bf16[256,512]{1,0:T(8,128)(2,1)}, u32[]{:S(2)}, u32[]{:S(2)}) collective-permute-start(bf16[256,512]{1,0:T(8,128)(2,1)} %add_convert_fusion.4), channel_id=1, source_target_pairs={{1,0},{4,1},{5,4},{8,5},{9,8},{12,9},{13,12},{3,2},{6,3},{7,6},{10... | collective-permute-start | bytes 786440 | tf_op jit(solution)/shard_map/ppermute | solution.py:13
Sparse Core Ops, SparseCore 0:
  99.3 39.3 reduce-scatter.3
  141.7 59.8 all-reduce.1
where the time goes:
time: 213 us; the launch traced here: 212 us
  waiting for transfers between devices  101 us (47%)
  matrix products  32.6 us (15%)
  starting transfers between devices  28.2 us (13%)
  local copies, waits for them, and re-layouts  20.5 us (10%)
  between operations  14.4 us (7%)
  other arithmetic  11.2 us (5%)
  loops' own time  3.92 us (2%)
    psum x1, waiting for transfers between devices, body(): weight_v = lax.psum(shard_v, ('ctx', 'sub')).astype(jnp.float32)  53.2 us
    unnamed x3, waiting for transfers between devices  28.5 us
    ppermute x12, starting transfers between devices, passed_along(): lax.ppermute(value, axis, [(source, source + steps) for source in range(f...  28.2 us
    ppermute x12, waiting for transfers between devices, passed_along(): lax.ppermute(value, axis, [(source, source + steps) for source in range(f...  19.3 us
    unnamed x25, local copies, waits for them, and re-layouts  17.9 us
    dot_general x2, matrix products, one_group(): jnp.einsum('htk,thd->kd', grad_scores, query_g, preferred_element_type=jn...  7.91 us
    dot_general x2, matrix products, one_group(): jnp.einsum('htk,kd->thd', grad_scores, key_g, preferred_element_type=jnp....  7.74 us
    sub x2, matrix products, one_group(): raised = jnp.where(allowed[None], jnp.exp(scores - largest), 0.0)  6.91 us
  transfers between devices with their start and end apart: 14, of which 7 were waited for; matrix products, arithmetic and copies ran while one was open for 9% of the time, Pallas kernels for 0%

commit v1 on v0

--- a/solution.py
+++ b/solution.py
@@ -103,7 +103,7 @@
         layer_input[0], grad_value, contract, preferred_element_type=jnp.float32
     )
     shard_v = lax.psum_scatter(term_v.astype(jnp.bfloat16), "fsdp", scatter_dimension=0, tiled=True)
-    weight_v = lax.psum(shard_v, ("ctx", "sub")).astype(jnp.float32)
+    weight_v = lax.psum(lax.psum(shard_v, "sub"), "ctx").astype(jnp.float32)
     token_scale = float(lax.axis_size("fsdp") * lax.axis_size(("ctx", "sub")) * block_rows) ** (
         -0.5
     )

time: 213 us -> 235 us (1.10)
  waiting for transfers between devices: 101 us -> 123 us
    unnamed x3 -> x4, waiting for transfers between devices: 28.5 us -> 39.5 us
    psum x1 -> x2, waiting for transfers between devices: 53.2 us -> 63.3 us  [body(): weight_v = lax.psum(lax.psum(shard_v, 'sub'), 'ctx').astype(jnp.float32)]
    unnamed x25 -> x27, local copies, waits for them, and re-layouts: 17.9 us -> 18.6 us
  transfers between devices with their start and end apart: 14 -> 15, of which waited for: 7 -> 8; matrix products, arithmetic and copies ran while one was open for 9% -> 7% of each run, Pallas kernels for 0% -> 0%
where the time goes in v1:
time: 235 us; the launch traced here: 234 us
  waiting for transfers between devices  123 us (52%)
  matrix products  32.6 us (14%)
  starting transfers between devices  28.3 us (12%)
  local copies, waits for them, and re-layouts  21.2 us (9%)
  between operations  14.1 us (6%)
  other arithmetic  10.4 us (4%)
  loops' own time  3.92 us (2%)
    psum x2, waiting for transfers between devices, body(): weight_v = lax.psum(lax.psum(shard_v, 'sub'), 'ctx').astype(jnp.float32)  63.3 us
    unnamed x4, waiting for transfers between devices  39.5 us
    ppermute x12, starting transfers between devices, passed_along(): lax.ppermute(value, axis, [(source, source + steps) for source in range(f...  28.2 us
    ppermute x12, waiting for transfers between devices, passed_along(): lax.ppermute(value, axis, [(source, source + steps) for source in range(f...  20.5 us
    unnamed x27, local copies, waits for them, and re-layouts  18.6 us
    dot_general x2, matrix products, one_group(): jnp.einsum('htk,thd->kd', grad_scores, query_g, preferred_element_type=jn...  7.9 us
    dot_general x2, matrix products, one_group(): jnp.einsum('htk,kd->thd', grad_scores, key_g, preferred_element_type=jnp....  7.74 us
    sub x2, matrix products, one_group(): raised = jnp.where(allowed[None], jnp.exp(scores - largest), 0.0)  6.94 us
  transfers between devices with their start and end apart: 15, of which 8 were waited for; matrix products, arithmetic and copies ran while one was open for 7% of the time, Pallas kernels for 0%

profile of v1, /device:TPU:0, one launch (start us, length us, event | category | flops | bytes accessed | tf_op | source)
XLA Modules:
  0.0 233.8 jit_solution(2710563306042020541)
XLA Ops:
  7.2 1.2 copy.68
  8.4 2.4 %collective-permute-start = (bf16[256,512]{0,1:T(8,128)(2,1)S(1)}, bf16[256,512]{0,1:T(8,128)(2,1)S(1)}, u32[]{:S(2)}, u32[]{:S(2)}) collective-permute-start(bf16[256,512]{0,1:T(8,128)(2,1)S(1)} %bitcast.186), channel_id=1, source_target_pairs={{0,1},{1,4},{4,5},{5,8},{8,9},{9,12},{12,13},{2,3},{3,6},{6,7},{7,... | collective-permute-start | bytes 786440 | tf_op jit(solution)/shard_map/ppermute | solution.py:13
  10.8 1.1 copy.71
  11.9 4.6 %collective-permute-start.3 = (bf16[256,512]{0,1:T(8,128)(2,1)S(1)}, bf16[256,512]{0,1:T(8,128)(2,1)S(1)}, u32[]{:S(2)}, u32[]{:S(2)}) collective-permute-start(bf16[256,512]{0,1:T(8,128)(2,1)S(1)} %bitcast.184), channel_id=1, source_target_pairs={{0,1},{1,4},{4,5},{5,8},{8,9},{9,12},{12,13},{2,3},{3,6},{6,7},{7,... | collective-permute-start | bytes 786440 | tf_op jit(solution)/shard_map/ppermute | solution.py:13
  16.5 2.2 collective-permute-start.1
  18.7 4.4 %collective-permute-start.4 = (bf16[256,512]{0,1:T(8,128)(2,1)S(1)}, bf16[256,512]{0,1:T(8,128)(2,1)S(1)}, u32[]{:S(2)}, u32[]{:S(2)}) collective-permute-start(bf16[256,512]{0,1:T(8,128)(2,1)S(1)} %collective-permute-done.3), channel_id=1, source_target_pairs={{0,1},{1,4},{4,5},{5,8},{8,9},{9,12},{12,13},{2,3},{3,6},{6,7},{7,... | collective-permute-start | bytes 786440 | tf_op jit(solution)/shard_map/ppermute | solution.py:13
  23.9 3.7 %collective-permute-start.2 = (bf16[256,512]{0,1:T(8,128)(2,1)S(1)}, bf16[256,512]{0,1:T(8,128)(2,1)}, u32[]{:S(2)}, u32[]{:S(2)}) collective-permute-start(bf16[256,512]{0,1:T(8,128)(2,1)S(1)} %collective-permute-done.1), channel_id=1, source_target_pairs={{0,1},{1,4},{4,5},{5,8},{8,9},{9,12},{12,13},{2,3},{3,6},{6,7},{7,... | collective-permute-start | bytes 786440 | tf_op jit(solution)/shard_map/ppermute | solution.py:13
  27.6 3.2 %collective-permute-start.5 = (bf16[256,512]{0,1:T(8,128)(2,1)S(1)}, bf16[256,512]{0,1:T(8,128)(2,1)S(1)}, u32[]{:S(2)}, u32[]{:S(2)}) collective-permute-start(bf16[256,512]{0,1:T(8,128)(2,1)S(1)} %collective-permute-done.4), channel_id=1, source_target_pairs={{0,1},{1,4},{4,5},{5,8},{8,9},{9,12},{12,13},{2,3},{3,6},{6,7},{7,... | collective-permute-start | bytes 786440 | tf_op jit(solution)/shard_map/ppermute | solution.py:13
  30.8 2.0 copy.73
  32.9 1.0 copy.70
  33.9 2.1 pad_maximum_fusion
  36.0 1.1 pad_maximum_fusion.1
  37.1 37.4 %while.15 = (s32[]{:T(128)}, bf16[2,256,2,256]{1,3,2,0:T(8,128)(2,1)}, f32[2,1024,256]{2,1,0:T(8,128)}, f32[2,1024,256]{2,1,0:T(8,128)}, s32[2]{0:T(128)S(1)}, /...) while((s32[]{:T(128)}, ...), condition=%wide.region_5.6_spmd.clone, body=%wide.region_1.5_spmd.clone.sunk | while | flops 1353977856 | bytes 29120200 | solution.py:54
  39.9 3.5 %fusion.90 = (f32[2,256]{1,0:T(2,128)S(1)}, f32[2,256,1024]{1,2,0:T(8,128)}) fusion(pred[256,1024]{0,1:T(8,128)(4,1)S(1)} %compare_and_fusion.2, bf16[256,2,2,256]{0,3,2,1:T(8,128)(2,1)} %get-tuple-element.287, s32[]{:T(128)S(6)} %select_n.34, bf16[1024,2,256]{0,2,1:T(8,128)(2,1)} %get-tuple-element.286), kind=kOutput, calls=%fused_computation.80.clone.1 | convolution fusion | flops 271057920 | bytes 3410944 | tf_op jit(solution)/shard_map/while/body/eval_jaxpr/sub | solution.py:43
  43.4 1.6 fusion.89
  45.0 3.9 %fusion.92 = f32[2,1024,256]{2,1,0:T(8,128)} fusion(f32[2,1024,256]{2,1,0:T(8,128)} %get-tuple-element.268, s32[]{:T(128)} %get-tuple-element.266, f32[1024,256,2]{1,0,2:T(8,128)S(1)} %fusion.89, bf16[256,2,2,256]{0,3,2,1:T(8,128)(2,1)} %get-tuple-element.287, s32[]{:T(128)S(6)} %select_n.34, f32[2,256,1024]{1,2,0:T(8,128)} %get-tuple-element.249, ...), kind=kOutput, calls=%fused_computation.14.clone.1 | convolution fusion | flops 272107008 | bytes 9703940 | tf_op jit(solution)/shard_map/while/body/eval_jaxpr/htk,thd->kd/dot_general | solution.py:50
  48.9 3.0 %fusion.93 = f32[2,1024,256]{2,1,0:T(8,128)} fusion(f32[2,1024,256]{2,1,0:T(8,128)} %get-tuple-element.269, s32[]{:T(128)} %get-tuple-element.266, bf16[256,2,2,256]{0,3,2,1:T(8,128)(2,1)} %get-tuple-element.289, s32[]{:T(128)S(6)} %select_n.34, f32[2,256,1024]{1,2,0:T(8,128)} %get-tuple-element.249, f32[2,256]{1,0:T(2,128)S(1)} %get-tuple-element.250), kind=kOutput, calls=%fused_computation.12.clone.1 | convolution fusion | flops 269484032 | bytes 3410436 | tf_op jit(solution)/shard_map/while/body/eval_jaxpr/htk,thd->kd/dot_general | solution.py:51
  51.9 3.9 %fusion.91 = bf16[2,256,2,256]{1,3,2,0:T(8,128)(2,1)} fusion(bf16[2,256,2,256]{1,3,2,0:T(8,128)(2,1)} %get-tuple-element.267, s32[]{:T(128)} %get-tuple-element.266, f32[1024,256,2]{1,0,2:T(8,128)S(1)} %fusion.89, bf16[1024,2,256]{0,2,1:T(8,128)(2,1)} %get-tuple-element.286, s32[]{:T(128)S(6)} %select_n.34, f32[2,256,1024]{1,2,0:T(8,128)} %get-tuple-element.249, ...), kind=kOutput, calls=%fused_computation.16.clone.1 | convolution fusion | flops 272107008 | bytes 9441796 | tf_op jit(solution)/shard_map/while/body/eval_jaxpr/htk,kd->thd/dot_general | solution.py:49
  58.6 3.5 %fusion.90 = (f32[2,256]{1,0:T(2,128)S(1)}, f32[2,256,1024]{1,2,0:T(8,128)}) fusion(pred[256,1024]{0,1:T(8,128)(4,1)S(1)} %compare_and_fusion.2, bf16[256,2,2,256]{0,3,2,1:T(8,128)(2,1)} %get-tuple-element.287, s32[]{:T(128)S(6)} %select_n.34, bf16[1024,2,256]{0,2,1:T(8,128)(2,1)} %get-tuple-element.286), kind=kOutput, calls=%fused_computation.80.clone.1 | convolution fusion | flops 271057920 | bytes 3410944 | tf_op jit(solution)/shard_map/while/body/eval_jaxpr/sub | solution.py:43
  62.1 1.6 fusion.89
  63.7 4.0 %fusion.92 = f32[2,1024,256]{2,1,0:T(8,128)} fusion(f32[2,1024,256]{2,1,0:T(8,128)} %get-tuple-element.268, s32[]{:T(128)} %get-tuple-element.266, f32[1024,256,2]{1,0,2:T(8,128)S(1)} %fusion.89, bf16[256,2,2,256]{0,3,2,1:T(8,128)(2,1)} %get-tuple-element.287, s32[]{:T(128)S(6)} %select_n.34, f32[2,256,1024]{1,2,0:T(8,128)} %get-tuple-element.249, ...), kind=kOutput, calls=%fused_computation.14.clone.1 | convolution fusion | flops 272107008 | bytes 9703940 | tf_op jit(solution)/shard_map/while/body/eval_jaxpr/htk,thd->kd/dot_general | solution.py:50
  67.6 3.0 %fusion.93 = f32[2,1024,256]{2,1,0:T(8,128)} fusion(f32[2,1024,256]{2,1,0:T(8,128)} %get-tuple-element.269, s32[]{:T(128)} %get-tuple-element.266, bf16[256,2,2,256]{0,3,2,1:T(8,128)(2,1)} %get-tuple-element.289, s32[]{:T(128)S(6)} %select_n.34, f32[2,256,1024]{1,2,0:T(8,128)} %get-tuple-element.249, f32[2,256]{1,0:T(2,128)S(1)} %get-tuple-element.250), kind=kOutput, calls=%fused_computation.12.clone.1 | convolution fusion | flops 269484032 | bytes 3410436 | tf_op jit(solution)/shard_map/while/body/eval_jaxpr/htk,thd->kd/dot_general | solution.py:51
  70.7 3.9 %fusion.91 = bf16[2,256,2,256]{1,3,2,0:T(8,128)(2,1)} fusion(bf16[2,256,2,256]{1,3,2,0:T(8,128)(2,1)} %get-tuple-element.267, s32[]{:T(128)} %get-tuple-element.266, f32[1024,256,2]{1,0,2:T(8,128)S(1)} %fusion.89, bf16[1024,2,256]{0,2,1:T(8,128)(2,1)} %get-tuple-element.286, s32[]{:T(128)S(6)} %select_n.34, f32[2,256,1024]{1,2,0:T(8,128)} %get-tuple-element.249, ...), kind=kOutput, calls=%fused_computation.16.clone.1 | convolution fusion | flops 272107008 | bytes 9441796 | tf_op jit(solution)/shard_map/while/body/eval_jaxpr/htk,kd->thd/dot_general | solution.py:49
  74.6 1.1 fusion.61
  75.6 1.3 collective-permute-start.9
  76.9 1.5 slice_bitcast_fusion.2
  78.5 1.2 collective-permute-done.9
  79.7 1.3 collective-permute-start.10
  81.1 6.3 %collective-permute-done.10 = bf16[256,512]{1,0:T(8,128)(2,1)S(1)} collective-permute-done((bf16[256,512]{1,0:T(8,128)(2,1)S(1)}, bf16[256,512]{1,0:T(8,128)(2,1)S(1)}, u32[]{:S(2)}, u32[]{:S(2)}) %collective-permute-start.10) | collective-permute-done | bytes 262176 | tf_op jit(solution)/shard_map/ppermute | solution.py:13
  87.5 1.3 collective-permute-start.11
  88.9 6.3 %collective-permute-done.11 = bf16[256,512]{1,0:T(8,128)(2,1)S(1)} collective-permute-done((bf16[256,512]{1,0:T(8,128)(2,1)S(1)}, bf16[256,512]{1,0:T(8,128)(2,1)S(1)}, u32[]{:S(2)}, u32[]{:S(2)}) %collective-permute-start.11) | collective-permute-done | bytes 262176 | tf_op jit(solution)/shard_map/ppermute | solution.py:13
  96.7 2.4 %copy.92 = bf16[2304,512]{1,0:T(8,128)(2,1)} copy(bf16[2304,512]{0,1:T(8,128)(2,1)S(1)} %fusion.57) | data formatting | bytes 4718592
  99.3 39.4 %reduce-scatter.4.cloned.1.call-done = bf16[1152,512]{1,0:T(8,128)(2,1)} async-done(((bf16[2304,512]{1,0:T(8,128)(2,1)}), bf16[1152,512]{1,0:T(8,128)(2,1)}) %reduce-scatter.4.cloned.1.call-update) | async-done | bytes 1179664
  138.7 2.4 %copy.93 = bf16[1152,512]{0,1:T(8,128)(2,1)} copy(bf16[1152,512]{1,0:T(8,128)(2,1)} %reduce-scatter.4.cloned.1.call-done) | data formatting | bytes 2359296
  141.2 1.1 fusion.60
  142.3 1.3 collective-permute-start.6
  143.6 1.5 slice_bitcast_fusion.5
  145.1 16.5 %all-reduce.3.cloned.1.call-done = bf16[1152,512]{0,1:T(8,128)(2,1)} async-done(((bf16[1152,512]{0,1:T(8,128)(2,1)}), bf16[1152,512]{0,1:T(8,128)(2,1)}) %all-reduce.3.cloned.1.call-update) | async-done | bytes 1179664 | tf_op jit(solution)/shard_map/psum | solution.py:106
  162.3 1.1 add_convert_fusion.5
  163.4 1.3 collective-permute-start.7
  164.8 2.1 collective-permute-done.7
  167.6 1.3 collective-permute-start.8
  169.0 1.0 copy.90
  170.8 4.6 %collective-permute-done.8 = bf16[256,512]{1,0:T(8,128)(2,1)} collective-permute-done((bf16[256,512]{1,0:T(8,128)(2,1)}, bf16[256,512]{1,0:T(8,128)(2,1)}, u32[]{:S(2)}, u32[]{:S(2)}) %collective-permute-start.8) | collective-permute-done | bytes 262176 | tf_op jit(solution)/shard_map/ppermute | solution.py:13
  175.4 1.7 fusion.59
  177.1 46.8 %all-reduce.5.cloned.1.call-done = bf16[1152,512]{0,1:T(8,128)(2,1)} async-done(((bf16[1152,512]{0,1:T(8,128)(2,1)}), bf16[1152,512]{0,1:T(8,128)(2,1)}) %all-reduce.5.cloned.1.call-update) | async-done | bytes 1179664 | tf_op jit(solution)/shard_map/psum | solution.py:106
  223.9 1.4 convert_multiply_fusion
  225.3 2.0 copy.87
  (54 shorter events, 7.0 us)
Async XLA Ops:
  7.2 88.7 %copy-start = (bf16[1,256,2304]{2,1,0:T(8,128)(2,1)S(1)}, bf16[1,256,2304]{2,1,0:T(8,128)(2,1)}, u32[]{:S(2)}) copy-start(bf16[1,256,2304]{2,1,0:T(8,128)(2,1)} %param.8) | copy-start | bytes 3538948
  7.2 25.7 %copy-start.5 = (bf16[1,256,1024]{2,1,0:T(8,128)(2,1)S(1)}, bf16[1,256,1024]{2,1,0:T(8,128)(2,1)}, u32[]{:S(2)}) copy-start(bf16[1,256,1024]{2,1,0:T(8,128)(2,1)} %param.9) | copy-start | bytes 1572868
  7.2 131.5 %reduce-scatter.4.cloned.1.call-start = ((), (), s32[]{:S(2)}) async-start(), calls=%async_computation.3 | async-start | bytes 3538944
  8.4 8.1 %collective-permute-start = (bf16[256,512]{0,1:T(8,128)(2,1)S(1)}, bf16[256,512]{0,1:T(8,128)(2,1)S(1)}, u32[]{:S(2)}, u32[]{:S(2)}) collective-permute-start(bf16[256,512]{0,1:T(8,128)(2,1)S(1)} %bitcast.186), channel_id=1, source_target_pairs={{0,1},{1,4},{4,5},{5,8},{8,9},{9,12},{12,13},{2,3},{3,6},{6,7},{7,... | collective-permute-start | bytes 786440 | tf_op jit(solution)/shard_map/ppermute | solution.py:13
  11.9 6.8 %collective-permute-start.3 = (bf16[256,512]{0,1:T(8,128)(2,1)S(1)}, bf16[256,512]{0,1:T(8,128)(2,1)S(1)}, u32[]{:S(2)}, u32[]{:S(2)}) collective-permute-start(bf16[256,512]{0,1:T(8,128)(2,1)S(1)} %bitcast.184), channel_id=1, source_target_pairs={{0,1},{1,4},{4,5},{5,8},{8,9},{9,12},{12,13},{2,3},{3,6},{6,7},{7,... | collective-permute-start | bytes 786440 | tf_op jit(solution)/shard_map/ppermute | solution.py:13
  16.5 7.4 %collective-permute-start.1 = (bf16[256,512]{0,1:T(8,128)(2,1)S(1)}, bf16[256,512]{0,1:T(8,128)(2,1)S(1)}, u32[]{:S(2)}, u32[]{:S(2)}) collective-permute-start(bf16[256,512]{0,1:T(8,128)(2,1)S(1)} %collective-permute-done), channel_id=1, source_target_pairs={{0,1},{1,4},{4,5},{5,8},{8,9},{9,12},{12,13},{2,3},{3,6},{6,7},{7,... | collective-permute-start | bytes 786440 | tf_op jit(solution)/shard_map/ppermute | solution.py:13
  18.7 8.9 %collective-permute-start.4 = (bf16[256,512]{0,1:T(8,128)(2,1)S(1)}, bf16[256,512]{0,1:T(8,128)(2,1)S(1)}, u32[]{:S(2)}, u32[]{:S(2)}) collective-permute-start(bf16[256,512]{0,1:T(8,128)(2,1)S(1)} %collective-permute-done.3), channel_id=1, source_target_pairs={{0,1},{1,4},{4,5},{5,8},{8,9},{9,12},{12,13},{2,3},{3,6},{6,7},{7,... | collective-permute-start | bytes 786440 | tf_op jit(solution)/shard_map/ppermute | solution.py:13
  23.9 10.0 %collective-permute-start.2 = (bf16[256,512]{0,1:T(8,128)(2,1)S(1)}, bf16[256,512]{0,1:T(8,128)(2,1)}, u32[]{:S(2)}, u32[]{:S(2)}) collective-permute-start(bf16[256,512]{0,1:T(8,128)(2,1)S(1)} %collective-permute-done.1), channel_id=1, source_target_pairs={{0,1},{1,4},{4,5},{5,8},{8,9},{9,12},{12,13},{2,3},{3,6},{6,7},{7,... | collective-permute-start | bytes 786440 | tf_op jit(solution)/shard_map/ppermute | solution.py:13
  27.6 8.4 %collective-permute-start.5 = (bf16[256,512]{0,1:T(8,128)(2,1)S(1)}, bf16[256,512]{0,1:T(8,128)(2,1)S(1)}, u32[]{:S(2)}, u32[]{:S(2)}) collective-permute-start(bf16[256,512]{0,1:T(8,128)(2,1)S(1)} %collective-permute-done.4), channel_id=1, source_target_pairs={{0,1},{1,4},{4,5},{5,8},{8,9},{9,12},{12,13},{2,3},{3,6},{6,7},{7,... | collective-permute-start | bytes 786440 | tf_op jit(solution)/shard_map/ppermute | solution.py:13
  75.6 4.0 %collective-permute-start.9 = (bf16[256,512]{1,0:T(8,128)(2,1)S(1)}, bf16[256,512]{1,0:T(8,128)(2,1)S(1)}, u32[]{:S(2)}, u32[]{:S(2)}) collective-permute-start(bf16[256,512]{1,0:T(8,128)(2,1)S(1)} %bitcast.190), channel_id=1, source_target_pairs={{1,0},{4,1},{5,4},{8,5},{9,8},{12,9},{13,12},{3,2},{6,3},{7,6},{10... | collective-permute-start | bytes 786440 | tf_op jit(solution)/shard_map/ppermute | solution.py:13
  79.7 7.7 %collective-permute-start.10 = (bf16[256,512]{1,0:T(8,128)(2,1)S(1)}, bf16[256,512]{1,0:T(8,128)(2,1)S(1)}, u32[]{:S(2)}, u32[]{:S(2)}) collective-permute-start(bf16[256,512]{1,0:T(8,128)(2,1)S(1)} %add_convert_fusion.2), channel_id=1, source_target_pairs={{1,0},{4,1},{5,4},{8,5},{9,8},{12,9},{13,12},{3,2},{6,3},{7,6},{10... | collective-permute-start | bytes 786440 | tf_op jit(solution)/shard_map/ppermute | solution.py:13
  87.5 7.7 %collective-permute-start.11 = (bf16[256,512]{1,0:T(8,128)(2,1)S(1)}, bf16[256,512]{1,0:T(8,128)(2,1)S(1)}, u32[]{:S(2)}, u32[]{:S(2)}) collective-permute-start(bf16[256,512]{1,0:T(8,128)(2,1)S(1)} %add_convert_fusion.1), channel_id=1, source_target_pairs={{1,0},{4,1},{5,4},{8,5},{9,8},{12,9},{13,12},{3,2},{6,3},{7,6},{10... | collective-permute-start | bytes 786440 | tf_op jit(solution)/shard_map/ppermute | solution.py:13
  88.9 6.3 %copy-start.1 = (f32[2,32,8,256]{3,2,0,1:T(8,128)}, f32[2,32,8,256]{3,2,0,1:T(8,128)S(1)}, u32[]{:S(2)}) copy-start(f32[2,32,8,256]{3,2,0,1:T(8,128)S(1)} %copy.105) | copy-start | bytes 1572868
  95.2 0.7 copy-start.3
  99.2 62.4 %all-reduce.3.cloned.1.call-start = ((), (), s32[]{:S(2)}) async-start(), calls=%async_computation.1 | async-start | bytes 2359296 | tf_op jit(solution)/shard_map/psum | solution.py:106
  141.1 82.8 %all-reduce.5.cloned.1.call-start = ((), (), s32[]{:S(2)}) async-start(), calls=%async_computation.2 | async-start | bytes 2359296 | tf_op jit(solution)/shard_map/psum | solution.py:106
  142.3 19.4 %collective-permute-start.6 = (bf16[256,512]{1,0:T(8,128)(2,1)S(1)}, bf16[256,512]{1,0:T(8,128)(2,1)S(1)}, u32[]{:S(2)}, u32[]{:S(2)}) collective-permute-start(bf16[256,512]{1,0:T(8,128)(2,1)S(1)} %bitcast.189), channel_id=1, source_target_pairs={{1,0},{4,1},{5,4},{8,5},{9,8},{12,9},{13,12},{3,2},{6,3},{7,6},{10... | collective-permute-start | bytes 786440 | tf_op jit(solution)/shard_map/ppermute | solution.py:13
  161.6 0.7 copy-start.7
  162.3 6.6 %copy-start.6 = (bf16[2,256,2,256]{1,3,2,0:T(8,128)(2,1)S(1)}, bf16[2,256,2,256]{1,3,2,0:T(8,128)(2,1)}, u32[]{:S(2)}) copy-start(bf16[2,256,2,256]{1,3,2,0:T(8,128)(2,1)} %get-tuple-element.58) | copy-start | bytes 1572868
  163.4 3.4 %collective-permute-start.7 = (bf16[256,512]{1,0:T(8,128)(2,1)S(1)}, bf16[256,512]{1,0:T(8,128)(2,1)S(1)}, u32[]{:S(2)}, u32[]{:S(2)}) collective-permute-start(bf16[256,512]{1,0:T(8,128)(2,1)S(1)} %add_convert_fusion.5), channel_id=1, source_target_pairs={{1,0},{4,1},{5,4},{8,5},{9,8},{12,9},{13,12},{3,2},{6,3},{7,6},{10... | collective-permute-start | bytes 786440 | tf_op jit(solution)/shard_map/ppermute | solution.py:13
  164.7 5.3 %copy-start.2 = (f32[2,32,8,256]{3,2,0,1:T(8,128)S(1)}, f32[2,32,8,256]{3,2,0,1:T(8,128)}, u32[]{:S(2)}) copy-start(f32[2,32,8,256]{3,2,0,1:T(8,128)} %copy-done.1) | copy-start | bytes 1572868
  164.7 5.3 %copy-start.4 = (bf16[256,512]{1,0:T(8,128)(2,1)S(1)}, bf16[256,512]{1,0:T(8,128)(2,1)}, u32[]{:S(2)}) copy-start(bf16[256,512]{1,0:T(8,128)(2,1)} %copy-done.3) | copy-start | bytes 786436
  167.6 7.7 %collective-permute-start.8 = (bf16[256,512]{1,0:T(8,128)(2,1)}, bf16[256,512]{1,0:T(8,128)(2,1)}, u32[]{:S(2)}, u32[]{:S(2)}) collective-permute-start(bf16[256,512]{1,0:T(8,128)(2,1)} %add_convert_fusion.4), channel_id=1, source_target_pairs={{1,0},{4,1},{5,4},{8,5},{9,8},{12,9},{13,12},{3,2},{6,3},{7,6},{10... | collective-permute-start | bytes 786440 | tf_op jit(solution)/shard_map/ppermute | solution.py:13
Sparse Core Ops, SparseCore 0:
  99.3 39.3 reduce-scatter.3
  141.7 19.8 all-reduce.2
  164.0 59.8 all-reduce.4
